TPU v7x, 32 devices: a whole 2x2x4 slice. The times are simulated.
32 devices in a mesh: groups: 2 (over y), bricks: 4 (over z), heads: 4 (over x, core).
Axes of the slice: x: 2, y: 2, z: 4, core: 2. Of those that a mesh axis runs over, the one named last changes fastest.
Arguments:
- voxel_feats: bfloat16 [4096, 1024], P(('groups', 'bricks'), 'heads'), parts along dimension 0, may hold values from -6 to 6
- face_open: int32 [8], P('groups'), parts along dimension 0, may hold values from 0 to 1
- pattern: int32 [8, 4], P('groups'), parts along dimension 0, may hold values from 0 to 1, as said below
- conv_weight: bfloat16 [27, 1024], P(None, 'heads'), may hold values from -1.25 to 1.25
- conv_bias: bfloat16 [1024], P('heads'), may hold values from -0.5 to 0.5
- gain_one: bfloat16 [1024], replicated, may hold values from 0.099609375 to 1.8984375
- query_weight: bfloat16 [1024, 1024], P(None, 'heads'), may hold values from -3 to 3
- key_weight: bfloat16 [1024, 1024], P(None, 'heads'), may hold values from -3 to 3
- value_weight: bfloat16 [1024, 1024], P(None, 'heads'), may hold values from -0.1875 to 0.1875
- out_weight: bfloat16 [1024, 1024], P('heads'), may hold values from -0.1875 to 0.1875
- gain_two: bfloat16 [1024], replicated, may hold values from 0.099609375 to 1.8984375
- up_weight: bfloat16 [1024, 4096], P(None, 'heads'), may hold values from -0.1875 to 0.1875
- down_weight: bfloat16 [4096, 1024], P('heads'), may hold values from -0.09375 to 0.09375
Outputs:
- block_out: bfloat16 [4096, 1024], P(('groups', 'bricks'), 'heads'), parts along dimension 0
There are 2 independent parts, one for each index of `groups`. A program takes and returns all parts, laid end to end along the dimension named above; an argument that names none is the same for every part. Nothing has to cross between parts.
Inputs may be any that keep to these rules, and one draw needn't show every extreme that they name: pattern is 0 or 1; every brick attends to itself; each query brick attends to 3 or more key bricks, and some query brick to all 4.
All inputs are finite; a program needn't handle non-finite values.
Results may differ from a plain program's by a relative error of at most 0.012.
Values may be sent and summed in bfloat16 or wider, within the bound.
No kernel may reach another device: no remote copies, remote signals or barrier semaphores. Data moves between devices by JAX's collectives and lax.ppermute only.
A program may use at most 64 MiB of HBM per device.

v0:
```python
import jax
import jax.numpy as jnp
from jax import lax
from jax.sharding import PartitionSpec as P

EDGE = 8
HEAD_DIM = 64
epsilon = 1e-05


def extended_2(value, sides, width):
    for axis, dim in sides:
        size, length = (lax.axis_size(axis), value.shape[dim])
        up = [(i, (i + 1) % size) for i in range(size - 1)]
        down = [(j, i) for i, j in up]
        last = lax.slice_in_dim(value, length - width, length, axis=dim)
        first = lax.slice_in_dim(value, 0, width, axis=dim)
        before = lax.ppermute(last, axis, up)
        after = lax.ppermute(first, axis, down)
        value = jnp.concatenate([before, value, after], axis=dim)
    return value


def layer_norm(inputs, gain_vec):
    values = inputs.astype(jnp.float32)
    center = values - jnp.mean(values, axis=-1, keepdims=True)
    spread = jnp.mean(center * center, axis=-1, keepdims=True)
    return center * lax.rsqrt(spread + epsilon) * gain_vec.astype(jnp.float32)


def depthwise(brick_vals, lower_face, upper_face, conv_weight, conv_bias):
    brick_count = brick_vals.shape[0]
    edge_len = brick_vals.shape[1]
    channels = brick_vals.shape[3]
    layers = jnp.concatenate([lower_face[:, None], brick_vals, upper_face[:, None]], axis=1)
    layers = layers.reshape(brick_count, edge_len + 2, edge_len, edge_len, channels)
    padded = jnp.pad(layers, ((0, 0), (0, 0), (1, 1), (1, 1), (0, 0)))
    weights = conv_weight.astype(jnp.float32)
    summed = jnp.zeros((brick_count, edge_len, edge_len, edge_len, channels), jnp.float32)
    for step_x in range(3):
        for step_y in range(3):
            for step_z in range(3):
                window = padded[
                    :,
                    step_x : step_x + edge_len,
                    step_y : step_y + edge_len,
                    step_z : step_z + edge_len,
                ]
                summed = summed + weights[step_x * 9 + step_y * 3 + step_z] * window
    return summed.reshape(brick_count * edge_len**3, channels) + conv_bias.astype(jnp.float32)


def shards(
    voxel_feats,
    face_open,
    pattern,
    conv_weight,
    conv_bias,
    gain_one,
    query_weight,
    key_weight,
    value_weight,
    out_weight,
    gain_two,
    up_weight,
    down_weight,
):
    row_count = voxel_feats.shape[0]
    local_width = voxel_feats.shape[1]
    face_rows = EDGE * EDGE
    brick_rows = EDGE * face_rows
    local_bricks = row_count // brick_rows
    brick_total = pattern.shape[0]
    first_brick = lax.axis_index("bricks") * local_bricks
    extended = extended_2(voxel_feats, (("bricks", 0),), face_rows)
    brick_vals = extended[face_rows : face_rows + row_count].astype(jnp.float32)
    brick_vals = brick_vals.reshape(local_bricks, EDGE, face_rows, local_width)
    lower_face = jnp.concatenate(
        [extended[:face_rows].astype(jnp.float32)[None], brick_vals[:-1, EDGE - 1]], axis=0
    )
    upper_face = jnp.concatenate(
        [brick_vals[1:, 0], extended[face_rows + row_count :].astype(jnp.float32)[None]], axis=0
    )
    brick_ids = first_brick + jnp.arange(local_bricks, dtype=jnp.int32)
    lower_open = jnp.where(brick_ids >= 1, jnp.take(face_open, brick_ids), 0)
    upper_open = jnp.where(
        brick_ids + 1 < brick_total,
        jnp.take(face_open, jnp.minimum(brick_ids + 1, brick_total - 1)),
        0,
    )
    lower_face = lower_face * lower_open.astype(jnp.float32)[:, None, None]
    upper_face = upper_face * upper_open.astype(jnp.float32)[:, None, None]
    conv_out = depthwise(brick_vals, lower_face, upper_face, conv_weight, conv_bias)
    stream = (voxel_feats.astype(jnp.float32) + conv_out).astype(jnp.bfloat16)
    stream_full = lax.all_gather(stream, "heads", axis=1, tiled=True)
    normed = layer_norm(stream_full, gain_one).astype(jnp.bfloat16)
    queries = jnp.dot(normed, query_weight, preferred_element_type=jnp.float32).astype(jnp.bfloat16)
    head_count = local_width // HEAD_DIM
    query_heads = queries.reshape(local_bricks, brick_rows, head_count, HEAD_DIM)
    score_scale = HEAD_DIM ** (-0.5)
    start_state = (
        jnp.full((local_bricks, head_count, brick_rows), -1e30, jnp.float32),
        jnp.zeros((local_bricks, head_count, brick_rows), jnp.float32),
        jnp.zeros((local_bricks, brick_rows, head_count, HEAD_DIM), jnp.float32),
    )

    def absorb(state_in, local_id, key_brick, fetch_pair):
        linked = pattern[first_brick + local_id, key_brick]

        def include(state_now):
            row_max, row_mass, weighted = state_now
            key_rows, value_rows = fetch_pair()
            keys_h = key_rows.reshape(brick_rows, head_count, HEAD_DIM)
            values_h = value_rows.reshape(brick_rows, head_count, HEAD_DIM)
            query_one = lax.dynamic_index_in_dim(query_heads, local_id, 0, keepdims=False)
            scores = (
                jnp.einsum("qhd,khd->hqk", query_one, keys_h, preferred_element_type=jnp.float32)
                * score_scale
            )
            max_old = lax.dynamic_index_in_dim(row_max, local_id, 0, keepdims=False)
            mass_old = lax.dynamic_index_in_dim(row_mass, local_id, 0, keepdims=False)
            sum_old = lax.dynamic_index_in_dim(weighted, local_id, 0, keepdims=False)
            max_new = jnp.maximum(max_old, jnp.max(scores, axis=-1))
            factor = jnp.exp(max_old - max_new)
            weights = jnp.exp(scores - max_new[:, :, None])
            mass_new = mass_old * factor + jnp.sum(weights, axis=-1)
            sum_new = sum_old * jnp.transpose(factor)[:, :, None] + jnp.einsum(
                "hqk,khd->qhd",
                weights.astype(jnp.bfloat16),
                values_h,
                preferred_element_type=jnp.float32,
            )
            return (
                lax.dynamic_update_index_in_dim(row_max, max_new, local_id, 0),
                lax.dynamic_update_index_in_dim(row_mass, mass_new, local_id, 0),
                lax.dynamic_update_index_in_dim(weighted, sum_new, local_id, 0),
            )

        return lax.cond(linked > 0, include, lambda state_now: state_now, state_in)

    keys_all = jnp.dot(normed, key_weight, preferred_element_type=jnp.float32).astype(jnp.bfloat16)
    values_all = jnp.dot(normed, value_weight, preferred_element_type=jnp.float32).astype(
        jnp.bfloat16
    )
    key_piece = lax.all_gather(keys_all, "bricks", axis=0, tiled=True)
    value_piece = lax.all_gather(values_all, "bricks", axis=0, tiled=True)
    piece_bricks = key_piece.shape[0] // brick_rows

    def visit(visit_idx, state_now):
        local_id = visit_idx // piece_bricks
        offset = visit_idx % piece_bricks

        def fetch_pair():
            return (
                lax.dynamic_slice_in_dim(key_piece, offset * brick_rows, brick_rows, 0),
                lax.dynamic_slice_in_dim(value_piece, offset * brick_rows, brick_rows, 0),
            )

        return absorb(state_now, local_id, offset, fetch_pair)

    result = lax.fori_loop(0, local_bricks * piece_bricks, visit, start_state)
    row_max, row_mass, weighted = result
    attended = (weighted / jnp.transpose(row_mass, (0, 2, 1))[:, :, :, None]).astype(jnp.bfloat16)
    attended = attended.reshape(row_count, local_width)
    partial_out = jnp.dot(attended, out_weight, preferred_element_type=jnp.float32)
    full_sum = lax.psum(partial_out.astype(jnp.bfloat16), "heads").astype(jnp.float32)
    stream_two_full = (stream_full.astype(jnp.float32) + full_sum).astype(jnp.bfloat16)
    stream_two = lax.dynamic_slice_in_dim(
        stream_two_full, lax.axis_index("heads") * local_width, local_width, 1
    )
    normed_two = layer_norm(stream_two_full, gain_two).astype(jnp.bfloat16)
    hidden = jax.nn.gelu(
        jnp.dot(normed_two, up_weight, preferred_element_type=jnp.float32), approximate=True
    ).astype(jnp.bfloat16)
    lowered = jnp.dot(hidden, down_weight, preferred_element_type=jnp.float32)
    mixed = lax.psum_scatter(
        lowered.astype(jnp.bfloat16), "heads", scatter_dimension=1, tiled=True
    ).astype(jnp.float32)
    return (stream_two.astype(jnp.float32) + mixed).astype(jnp.bfloat16)


def solution(mesh):
    return jax.shard_map(
        shards,
        mesh=mesh,
        in_specs=(
            P(("groups", "bricks"), "heads"),
            P("groups"),
            P("groups", None),
            P(None, "heads"),
            P("heads"),
            P(),
            P(None, "heads"),
            P(None, "heads"),
            P(None, "heads"),
            P("heads", None),
            P(),
            P(None, "heads"),
            P("heads", None),
        ),
        out_specs=P(("groups", "bricks"), "heads"),
        check_vma=False,
    )
```

profile of v0, /device:TPU:0, one launch (start us, length us, event | category | flops | bytes accessed | tf_op | source)
XLA Modules:
  0.0 208.5 jit_solution(12115050096938499187)
XLA Ops:
  7.5 1.3 collective-permute-start.1
  8.8 5.6 %collective-permute-start = (bf16[64,256]{1,0:T(8,128)(2,1)S(1)}, bf16[64,256]{1,0:T(8,128)(2,1)S(1)}, u32[]{:S(2)}, u32[]{:S(2)}) collective-permute-start(bf16[64,256]{1,0:T(8,128)(2,1)S(1)} %get-tuple-element.350), channel_id=1, source_target_pairs={{0,4},{4,8},{8,12},{1,5},{5,9},{9,13},{2,6},{6,10},{10,14},{3,7},{... | collective-permute-start | bytes 98312 | tf_op jit(solution)/shard_map/ppermute | solution.py:18
  16.2 1.4 fusion.98
  20.9 1.6 fusion.57
  23.4 17.6 %all-gather.4.cloned.1.call-done = bf16[512,1024]{1,0:T(8,128)(2,1)} async-done(((bf16[512,256]{1,0:T(8,128)(2,1)}), bf16[512,1024]{1,0:T(8,128)(2,1)}) %all-gather.4.cloned.1.call-update) | async-done | bytes 1048592 | tf_op jit(solution)/shard_map/all_gather | solution.py:95
  41.0 1.5 convert_reduce_fusion
  42.5 1.6 fusion.25
  44.2 2.3 %convolution_convert_fusion.4 = bf16[512,256]{1,0:T(8,128)(2,1)} fusion(bf16[1024,256]{1,0:T(8,128)(2,1)} %param.24, bf16[512,1024]{1,0:T(8,128)(2,1)S(1)} %copy-done.1, f32[1024]{0:T(1024)S(1)} %convert_element_type.108, f32[512]{0:T(512)S(1)} %add_rsqrt_fusion.1, f32[512]{0:T(512)S(1)} %broadcast_multiply_fusion.1), kind=kOutput, calls=%fused_computation.61 | convolution fusion | flops 271187968 | bytes 1843200 | tf_op jit(solution)/shard_map/dot_general | solution.py:141
  46.5 2.3 %convolution_convert_fusion.2 = bf16[512,256]{1,0:T(8,128)(2,1)} fusion(bf16[1024,256]{1,0:T(8,128)(2,1)} %param.25, bf16[512,1024]{1,0:T(8,128)(2,1)S(1)} %copy-done.1, f32[1024]{0:T(1024)S(1)} %convert_element_type.108, f32[512]{0:T(512)S(1)} %add_rsqrt_fusion.1, f32[512]{0:T(512)S(1)} %broadcast_multiply_fusion.1), kind=kOutput, calls=%fused_computation.59 | convolution fusion | flops 271187968 | bytes 1843200 | tf_op jit(solution)/shard_map/dot_general | solution.py:142
  48.8 1.7 convolution_convert_fusion.3
  50.6 24.0 %all-gather.6.cloned.1.call-done = bf16[2048,256]{1,0:T(8,128)(2,1)} async-done(((bf16[512,256]{1,0:T(8,128)(2,1)}), bf16[2048,256]{1,0:T(8,128)(2,1)}) %all-gather.6.cloned.1.call-update) | async-done | bytes 1048592 | tf_op jit(solution)/shard_map/all_gather | solution.py:145
  74.5 2.3 %copy.15 = bf16[2048,256]{0,1:T(8,128)(2,1)} copy(bf16[2048,256]{1,0:T(8,128)(2,1)} %all-gather.6.cloned.1.call-done) | data formatting | bytes 2097152 | tf_op jit(solution)/shard_map/while | solution.py:161
  76.8 26.8 %all-gather.8.cloned.1.call-done = bf16[2048,256]{1,0:T(8,128)(2,1)} async-done(((bf16[512,256]{1,0:T(8,128)(2,1)}), bf16[2048,256]{1,0:T(8,128)(2,1)}) %all-gather.8.cloned.1.call-update) | async-done | bytes 1048592 | tf_op jit(solution)/shard_map/all_gather | solution.py:146
  103.6 2.3 %copy.16 = bf16[2048,256]{0,1:T(8,128)(2,1)} copy(bf16[2048,256]{1,0:T(8,128)(2,1)} %all-gather.8.cloned.1.call-done) | data formatting | bytes 2097152 | tf_op jit(solution)/shard_map/while | solution.py:161
  105.9 22.0 %while.21 = (s32[]{:T(128)}, f32[1,4,512]{2,1,0:T(4,128)S(1)}, f32[1,4,512]{2,1,0:T(4,128)S(1)}, f32[1,512,4,64]{1,3,2,0:T(8,128)S(1)}, s32[]{:T(128)}, /*index=...) while((s32[]{:T(128)}, f32[1,4,512]{2,1,0:T(4,128)S(1)}, ...), condition=%wide.region_7.8_spmd, body=%wide.region_2.0_spmd.sunk | while | flops 277094432 | bytes 15589916 | solution.py:161
  106.0 1.3 dynamic_slice.33
  107.9 3.5 %conditional.2 = ((f32[1,4,512]{2,1,0:T(4,128)S(1)}, f32[1,4,512]{2,1,0:T(4,128)S(1)}, f32[1,512,4,64]{1,3,2,0:T(8,128)S(1)})) conditional(s32[]{:T(128)} %bitcast.111, (f32[1,4,512]{2,1,0:T(4,128)S(1)}, f32[1,4,512]{2,1,0:T(4,128)S(1)}, f32[1,512,4,64]{1,3,2,0:T(8,128)S(1)}) %tuple.92, (s32[]{:T(128)}, bf16[2048,256]{0,1:T(8,128)(2,1)}, ...), branch_computations={%region_3.3_spmd, %region_4.6_spmd} | conditional | flops 277094400 | bytes 15589458 | solution.py:139
  107.9 1.1 constant_dynamic-slice_fusion
  111.5 1.3 dynamic_slice.33
  113.4 3.5 %conditional.2 = ((f32[1,4,512]{2,1,0:T(4,128)S(1)}, f32[1,4,512]{2,1,0:T(4,128)S(1)}, f32[1,512,4,64]{1,3,2,0:T(8,128)S(1)})) conditional(s32[]{:T(128)} %bitcast.111, (f32[1,4,512]{2,1,0:T(4,128)S(1)}, f32[1,4,512]{2,1,0:T(4,128)S(1)}, f32[1,512,4,64]{1,3,2,0:T(8,128)S(1)}) %tuple.92, (s32[]{:T(128)}, bf16[2048,256]{0,1:T(8,128)(2,1)}, ...), branch_computations={%region_3.3_spmd, %region_4.6_spmd} | conditional | flops 277094400 | bytes 15589458 | solution.py:139
  113.4 1.1 constant_dynamic-slice_fusion
  117.0 1.3 dynamic_slice.33
  118.9 3.5 %conditional.2 = ((f32[1,4,512]{2,1,0:T(4,128)S(1)}, f32[1,4,512]{2,1,0:T(4,128)S(1)}, f32[1,512,4,64]{1,3,2,0:T(8,128)S(1)})) conditional(s32[]{:T(128)} %bitcast.111, (f32[1,4,512]{2,1,0:T(4,128)S(1)}, f32[1,4,512]{2,1,0:T(4,128)S(1)}, f32[1,512,4,64]{1,3,2,0:T(8,128)S(1)}) %tuple.92, (s32[]{:T(128)}, bf16[2048,256]{0,1:T(8,128)(2,1)}, ...), branch_computations={%region_3.3_spmd, %region_4.6_spmd} | conditional | flops 277094400 | bytes 15589458 | solution.py:139
  118.9 1.1 constant_dynamic-slice_fusion
  122.5 1.3 dynamic_slice.33
  124.4 3.5 %conditional.2 = ((f32[1,4,512]{2,1,0:T(4,128)S(1)}, f32[1,4,512]{2,1,0:T(4,128)S(1)}, f32[1,512,4,64]{1,3,2,0:T(8,128)S(1)})) conditional(s32[]{:T(128)} %bitcast.111, (f32[1,4,512]{2,1,0:T(4,128)S(1)}, f32[1,4,512]{2,1,0:T(4,128)S(1)}, f32[1,512,4,64]{1,3,2,0:T(8,128)S(1)}) %tuple.92, (s32[]{:T(128)}, bf16[2048,256]{0,1:T(8,128)(2,1)}, ...), branch_computations={%region_3.3_spmd, %region_4.6_spmd} | conditional | flops 277094400 | bytes 15589458 | solution.py:139
  128.0 2.6 %convolution_convert_fusion.1 = bf16[512,1024]{1,0:T(8,128)(2,1)} fusion(bf16[512,256]{0,1:T(8,128)(2,1)S(1)} %bitcast.116, bf16[256,1024]{1,0:T(8,128)(2,1)} %param.26), kind=kOutput, calls=%fused_computation.58 | convolution fusion | flops 268959744 | bytes 1835008 | tf_op jit(solution)/shard_map/dot_general | solution.py:165
  130.7 35.7 %all-reduce.3.cloned.1.call-done = bf16[512,1024]{1,0:T(8,128)(2,1)} async-done(((bf16[512,1024]{1,0:T(8,128)(2,1)}), bf16[512,1024]{1,0:T(8,128)(2,1)}) %all-reduce.3.cloned.1.call-update) | async-done | bytes 1048592 | tf_op jit(solution)/shard_map/psum | solution.py:166
  166.4 1.6 convert_reduce_fusion.1
  169.4 5.4 %convolution_convert_fusion = bf16[512,1024]{1,0:T(8,128)(2,1)} fusion(bf16[1024,1024]{1,0:T(8,128)(2,1)S(1)} %copy-done, bf16[1024,1024]{1,0:T(8,128)(2,1)} %param.28, bf16[512,1024]{1,0:T(8,128)(2,1)} %copy-done.3, f32[1024]{0:T(1024)S(1)} %convert_element_type.119, f32[512]{0:T(512)S(1)} %add_rsqrt_fusion, f32[512]{0:T(512)S(1)} %broadcast_multiply_fusion), kind=kOutput, calls=%fused_computation.57 | convolution fusion | flops 2155347968 | bytes 6299648 | tf_op jit(solution)/shard_map/dot_general | solution.py:175
  174.8 25.4 %reduce-scatter.2.cloned.1.call-done = bf16[512,256]{1,0:T(8,128)(2,1)} async-done(((bf16[512,1024]{1,0:T(8,128)(2,1)}), bf16[512,256]{1,0:T(8,128)(2,1)}) %reduce-scatter.2.cloned.1.call-update) | async-done | bytes 262160 | tf_op jit(solution)/shard_map/reduce_scatter | solution.py:176
  200.2 1.8 add_convert_fusion
  (67 shorter events, 18.1 us)
Async XLA Ops:
  6.5 162.8 %copy-start = (bf16[1024,1024]{1,0:T(8,128)(2,1)S(1)}, bf16[1024,1024]{1,0:T(8,128)(2,1)}, u32[]{:S(2)}) copy-start(bf16[1024,1024]{1,0:T(8,128)(2,1)} %param.29) | copy-start | bytes 6291460
  6.5 34.4 %all-gather.4.cloned.1.call-start = ((), (), s32[]{:S(2)}) async-start(), calls=%async_computation.1 | async-start | bytes 1310720 | tf_op jit(solution)/shard_map/all_gather | solution.py:95
  7.5 13.1 %collective-permute-start.1 = (bf16[64,256]{1,0:T(8,128)(2,1)S(1)}, bf16[64,256]{1,0:T(8,128)(2,1)S(1)}, u32[]{:S(2)}, u32[]{:S(2)}) collective-permute-start(bf16[64,256]{1,0:T(8,128)(2,1)S(1)} %get-tuple-element.351), channel_id=1, source_target_pairs={{4,0},{8,4},{12,8},{5,1},{9,5},{13,9},{6,2},{10,6},{14,10},{7,3},{... | collective-permute-start | bytes 98312 | tf_op jit(solution)/shard_map/ppermute | solution.py:19
  8.8 11.8 %collective-permute-start = (bf16[64,256]{1,0:T(8,128)(2,1)S(1)}, bf16[64,256]{1,0:T(8,128)(2,1)S(1)}, u32[]{:S(2)}, u32[]{:S(2)}) collective-permute-start(bf16[64,256]{1,0:T(8,128)(2,1)S(1)} %get-tuple-element.350), channel_id=1, source_target_pairs={{0,4},{4,8},{8,12},{1,5},{5,9},{9,13},{2,6},{6,10},{10,14},{3,7},{... | collective-permute-start | bytes 98312 | tf_op jit(solution)/shard_map/ppermute | solution.py:18
  20.9 1.6 copy-start.4
  20.9 2.5 %copy-start.5 = (bf16[1024]{0:T(1024)(128)(2,1)S(1)}, bf16[1024]{0:T(1024)(128)(2,1)}, u32[]{:S(2)}) copy-start(bf16[1024]{0:T(1024)(128)(2,1)} %param.22) | copy-start | bytes 6148
  23.3 51.2 %all-gather.6.cloned.1.call-start = ((), (), s32[]{:S(2)}) async-start(), calls=%async_computation.2 | async-start | bytes 1310720 | tf_op jit(solution)/shard_map/all_gather | solution.py:145
  41.0 3.2 %copy-start.1 = (bf16[512,1024]{1,0:T(8,128)(2,1)S(1)}, bf16[512,1024]{1,0:T(8,128)(2,1)}, u32[]{:S(2)}) copy-start(bf16[512,1024]{1,0:T(8,128)(2,1)} %all-gather.4.cloned.1.call-done) | copy-start | bytes 3145732
  46.4 57.1 %all-gather.8.cloned.1.call-start = ((), (), s32[]{:S(2)}) async-start(), calls=%async_computation.3 | async-start | bytes 1310720 | tf_op jit(solution)/shard_map/all_gather | solution.py:146
  48.8 117.6 %all-reduce.3.cloned.1.call-start = ((), (), s32[]{:S(2)}) async-start(), calls=%async_computation.4 | async-start | bytes 2097152 | tf_op jit(solution)/shard_map/psum | solution.py:166
  127.9 2.7 %copy-start.6 = (bf16[1024]{0:T(1024)(128)(2,1)S(1)}, bf16[1024]{0:T(1024)(128)(2,1)}, u32[]{:S(2)}) copy-start(bf16[1024]{0:T(1024)(128)(2,1)} %param.27) | copy-start | bytes 6148
  128.0 38.3 %copy-start.2 = (bf16[512,1024]{1,0:T(8,128)(2,1)S(1)}, bf16[512,1024]{1,0:T(8,128)(2,1)}, u32[]{:S(2)}) copy-start(bf16[512,1024]{1,0:T(8,128)(2,1)} %all-gather.4.cloned.1.call-done) | copy-start | bytes 3145732
  130.6 69.5 %reduce-scatter.2.cloned.1.call-start = ((), (), s32[]{:S(2)}) async-start(), calls=%async_computation.5 | async-start | bytes 1310720 | tf_op jit(solution)/shard_map/reduce_scatter | solution.py:176
  168.0 1.0 copy-start.3
Sparse Core Ops, SparseCore 0:
  23.4 17.5 all-gather.3
  46.6 27.9 all-gather.5
  76.1 27.4 all-gather.7
  130.7 35.5 all-reduce.2
  174.9 25.2 reduce-scatter.1
where the time goes:
time: 209 us; the launch traced here: 208 us
  waiting for transfers between devices  129 us (62%)
  matrix products  21 us (10%)
  local copies, waits for them, and re-layouts  19.2 us (9%)
  between operations  14.6 us (7%)
  other arithmetic  14.3 us (7%)
  starting transfers between devices  7.01 us (3%)
  loops' own time  2.85 us (1%)
    psum x1, waiting for transfers between devices, shards(): lax.psum(partial_out.astype(jnp.bfloat16), 'heads').astype(jnp.float32)  35.7 us
    all_gather x1, waiting for transfers between devices, shards(): value_piece = lax.all_gather(values_all, 'bricks', axis=0, tiled=True)  26.8 us
    reduce_scatter x1, waiting for transfers between devices, shards(): lax.psum_scatter(lowered.astype(jnp.bfloat16), 'heads', scatter_dimension...  25.4 us
    all_gather x1, waiting for transfers between devices, shards(): key_piece = lax.all_gather(keys_all, 'bricks', axis=0, tiled=True)  24 us
    all_gather x1, waiting for transfers between devices, shards(): stream_full = lax.all_gather(stream, 'heads', axis=1, tiled=True)  17.6 us
    ppermute x1, starting transfers between devices, extended_2(): before = lax.ppermute(last, axis, up)  5.56 us
    dot_general x1, matrix products, shards(): lowered = jnp.dot(hidden, down_weight, preferred_element_type=jnp.float32)  5.37 us
    dynamic_slice x4, local copies, waits for them, and re-layouts, absorb(): linked = pattern[first_brick + local_id, key_brick]  5.15 us
  transfers between devices with their start and end apart: 7, of which 5 were waited for; matrix products, arithmetic and copies ran while one was open for 5% of the time, Pallas kernels for 0%

commit v1 on v0

--- a/solution.py
+++ b/solution.py
@@ -6,6 +6,11 @@
 EDGE = 8
 HEAD_DIM = 64
 epsilon = 1e-05
+_clear_knots = lambda block_in, z_in, mesh_dim: jnp.split(
+    lax.all_gather(jnp.concatenate([block_in, z_in], 1), axis_name=mesh_dim, axis=0, tiled=True),
+    [block_in.shape[1]],
+    1,
+)
 
 
 def extended_2(value, sides, width):
@@ -142,8 +147,7 @@
     values_all = jnp.dot(normed, value_weight, preferred_element_type=jnp.float32).astype(
         jnp.bfloat16
     )
-    key_piece = lax.all_gather(keys_all, "bricks", axis=0, tiled=True)
-    value_piece = lax.all_gather(values_all, "bricks", axis=0, tiled=True)
+    key_piece, value_piece = _clear_knots(keys_all, z_in=values_all, mesh_dim="bricks")
     piece_bricks = key_piece.shape[0] // brick_rows
 
     def visit(visit_idx, state_now):

time: 209 us -> 199 us (0.952)
  waiting for transfers between devices: 129 us -> 122 us
  matrix products: 21 us -> 18.9 us
    all_gather x2 -> x1, waiting for transfers between devices: 50.7 us -> 44.3 us  [lax.all_gather(jnp.concatenate([block_in, z_in], 1), axis_name=mesh_dim,...]
    while x2 -> x0, local copies, waits for them, and re-layouts: 4.55 us -> none  [shards(): result = lax.fori_loop(0, local_bricks * piece_bricks, visit, start_state)]
    split x0 -> x1, local copies, waits for them, and re-layouts: none -> 3.15 us  [jnp.split(lax.all_gather(jnp.concatenate([block_in, z_in], 1), axis_name=...]
  transfers between devices with their start and end apart: 7 -> 6, of which waited for: 5 -> 4; matrix products, arithmetic and copies ran while one was open for 5% -> 3% of each run, Pallas kernels for 0% -> 0%
where the time goes in v1:
time: 199 us; the launch traced here: 198 us
  waiting for transfers between devices  122 us (61%)
  matrix products  18.9 us (9%)
  local copies, waits for them, and re-layouts  17.8 us (9%)
  other arithmetic  15.2 us (8%)
  between operations  14.6 us (7%)
  starting transfers between devices  6.97 us (4%)
  loops' own time  2.62 us (1%)
    all_gather x1, waiting for transfers between devices, lax.all_gather(jnp.concatenate([block_in, z_in], 1), axis_name=mesh_dim,...  44.3 us
    psum x1, waiting for transfers between devices, shards(): lax.psum(partial_out.astype(jnp.bfloat16), 'heads').astype(jnp.float32)  34.9 us
    reduce_scatter x1, waiting for transfers between devices, shards(): lax.psum_scatter(lowered.astype(jnp.bfloat16), 'heads', scatter_dimension...  25.4 us
    all_gather x1, waiting for transfers between devices, shards(): stream_full = lax.all_gather(stream, 'heads', axis=1, tiled=True)  17.6 us
    ppermute x1, starting transfers between devices, extended_2(): before = lax.ppermute(last, axis, up)  5.56 us
    dot_general x1, matrix products, shards(): lowered = jnp.dot(hidden, down_weight, preferred_element_type=jnp.float32)  5.37 us
    dynamic_slice x4, local copies, waits for them, and re-layouts, absorb(): linked = pattern[first_brick + local_id, key_brick]  5.09 us
    dynamic_slice x4, local copies, waits for them, and re-layouts, fetch_pair(): lax.dynamic_slice_in_dim(value_piece, offset * brick_rows, brick_rows, 0)  4.29 us
  transfers between devices with their start and end apart: 6, of which 4 were waited for; matrix products, arithmetic and copies ran while one was open for 3% of the time, Pallas kernels for 0%

profile of v1, /device:TPU:0, one launch (start us, length us, event | category | flops | bytes accessed | tf_op | source)
XLA Modules:
  0.0 198.4 jit_solution(14664629531475574651)
XLA Ops:
  7.5 1.3 collective-permute-start.1
  8.8 5.6 %collective-permute-start = (bf16[64,256]{1,0:T(8,128)(2,1)S(1)}, bf16[64,256]{1,0:T(8,128)(2,1)S(1)}, u32[]{:S(2)}, u32[]{:S(2)}) collective-permute-start(bf16[64,256]{1,0:T(8,128)(2,1)S(1)} %get-tuple-element.343), channel_id=1, source_target_pairs={{0,4},{4,8},{8,12},{1,5},{5,9},{9,13},{2,6},{6,10},{10,14},{3,7},{... | collective-permute-start | bytes 98312 | tf_op jit(solution)/shard_map/ppermute | solution.py:23
  14.3 1.0 fusion.97
  16.2 1.4 fusion.99
  18.2 1.0 convert.1
  20.8 1.6 fusion.57
  23.3 17.6 %all-gather.3.cloned.1.call-done = bf16[512,1024]{1,0:T(8,128)(2,1)} async-done(((bf16[512,256]{1,0:T(8,128)(2,1)}), bf16[512,1024]{1,0:T(8,128)(2,1)}) %all-gather.3.cloned.1.call-update) | async-done | bytes 1048592 | tf_op jit(solution)/shard_map/all_gather | solution.py:100
  40.9 1.5 convert_reduce_fusion
  42.4 1.7 fusion.25
  44.1 1.7 convolution_convert_fusion.3
  47.5 1.7 convolution_convert_fusion.2
  49.3 44.3 %all-gather.5.cloned.1.call-done = bf16[2048,512]{0,1:T(8,128)(2,1)} async-done(((bf16[512,512]{0,1:T(8,128)(2,1)}), bf16[2048,512]{0,1:T(8,128)(2,1)}) %all-gather.5.cloned.1.call-update) | async-done | bytes 2097168 | tf_op jit(solution)/shard_map/all_gather | solution.py:10
  93.6 3.2 %fusion.95 = (bf16[2048,256]{0,1:T(8,128)(2,1)}, bf16[2048,256]{0,1:T(8,128)(2,1)}) fusion(bf16[2048,512]{0,1:T(8,128)(2,1)} %all-gather.5.cloned.1.call-done), kind=kLoop, calls=%fused_computation.140 | loop fusion | bytes 4194304 | tf_op jit(solution)/shard_map/split | solution.py:9
  96.8 21.7 %while.21 = (s32[]{:T(128)}, f32[1,4,512]{2,1,0:T(4,128)S(1)}, f32[1,4,512]{2,1,0:T(4,128)S(1)}, f32[1,512,4,64]{1,3,2,0:T(8,128)S(1)}, s32[]{:T(128)}, /*index=...) while((s32[]{:T(128)}, f32[1,4,512]{2,1,0:T(4,128)S(1)}, ...), condition=%wide.region_7.8_spmd, body=%wide.region_2.0_spmd.sunk | while | flops 277094432 | bytes 15589916 | solution.py:165
  96.8 1.3 dynamic_slice.33
  98.7 3.5 %conditional.2 = ((f32[1,4,512]{2,1,0:T(4,128)S(1)}, f32[1,4,512]{2,1,0:T(4,128)S(1)}, f32[1,512,4,64]{1,3,2,0:T(8,128)S(1)})) conditional(s32[]{:T(128)} %bitcast.111, (f32[1,4,512]{2,1,0:T(4,128)S(1)}, f32[1,4,512]{2,1,0:T(4,128)S(1)}, f32[1,512,4,64]{1,3,2,0:T(8,128)S(1)}) %tuple.92, (s32[]{:T(128)}, bf16[2048,256]{0,1:T(8,128)(2,1)}, ...), branch_computations={%region_3.3_spmd, %region_4.6_spmd} | conditional | flops 277094400 | bytes 15589458 | solution.py:144
  98.7 1.1 constant_dynamic-slice_fusion
  102.2 1.3 dynamic_slice.33
  104.1 3.5 %conditional.2 = ((f32[1,4,512]{2,1,0:T(4,128)S(1)}, f32[1,4,512]{2,1,0:T(4,128)S(1)}, f32[1,512,4,64]{1,3,2,0:T(8,128)S(1)})) conditional(s32[]{:T(128)} %bitcast.111, (f32[1,4,512]{2,1,0:T(4,128)S(1)}, f32[1,4,512]{2,1,0:T(4,128)S(1)}, f32[1,512,4,64]{1,3,2,0:T(8,128)S(1)}) %tuple.92, (s32[]{:T(128)}, bf16[2048,256]{0,1:T(8,128)(2,1)}, ...), branch_computations={%region_3.3_spmd, %region_4.6_spmd} | conditional | flops 277094400 | bytes 15589458 | solution.py:144
  104.1 1.1 constant_dynamic-slice_fusion
  107.7 1.3 dynamic_slice.33
  109.5 3.5 %conditional.2 = ((f32[1,4,512]{2,1,0:T(4,128)S(1)}, f32[1,4,512]{2,1,0:T(4,128)S(1)}, f32[1,512,4,64]{1,3,2,0:T(8,128)S(1)})) conditional(s32[]{:T(128)} %bitcast.111, (f32[1,4,512]{2,1,0:T(4,128)S(1)}, f32[1,4,512]{2,1,0:T(4,128)S(1)}, f32[1,512,4,64]{1,3,2,0:T(8,128)S(1)}) %tuple.92, (s32[]{:T(128)}, bf16[2048,256]{0,1:T(8,128)(2,1)}, ...), branch_computations={%region_3.3_spmd, %region_4.6_spmd} | conditional | flops 277094400 | bytes 15589458 | solution.py:144
  109.5 1.1 constant_dynamic-slice_fusion
  113.1 1.3 dynamic_slice.33
  115.0 3.5 %conditional.2 = ((f32[1,4,512]{2,1,0:T(4,128)S(1)}, f32[1,4,512]{2,1,0:T(4,128)S(1)}, f32[1,512,4,64]{1,3,2,0:T(8,128)S(1)})) conditional(s32[]{:T(128)} %bitcast.111, (f32[1,4,512]{2,1,0:T(4,128)S(1)}, f32[1,4,512]{2,1,0:T(4,128)S(1)}, f32[1,512,4,64]{1,3,2,0:T(8,128)S(1)}) %tuple.92, (s32[]{:T(128)}, bf16[2048,256]{0,1:T(8,128)(2,1)}, ...), branch_computations={%region_3.3_spmd, %region_4.6_spmd} | conditional | flops 277094400 | bytes 15589458 | solution.py:144
  115.0 1.1 constant_dynamic-slice_fusion
  118.6 2.6 %convolution_convert_fusion.1 = bf16[512,1024]{1,0:T(8,128)(2,1)} fusion(bf16[512,256]{0,1:T(8,128)(2,1)S(1)} %bitcast.116, bf16[256,1024]{1,0:T(8,128)(2,1)} %param.26), kind=kOutput, calls=%fused_computation.58 | convolution fusion | flops 268959744 | bytes 1835008 | tf_op jit(solution)/shard_map/dot_general | solution.py:169
  121.3 34.9 %all-reduce.3.cloned.1.call-done = bf16[512,1024]{1,0:T(8,128)(2,1)} async-done(((bf16[512,1024]{1,0:T(8,128)(2,1)}), bf16[512,1024]{1,0:T(8,128)(2,1)}) %all-reduce.3.cloned.1.call-update) | async-done | bytes 1048592 | tf_op jit(solution)/shard_map/psum | solution.py:170
  156.2 1.6 convert_reduce_fusion.1
  159.2 5.4 %convolution_convert_fusion = bf16[512,1024]{1,0:T(8,128)(2,1)} fusion(bf16[1024,1024]{1,0:T(8,128)(2,1)S(1)} %copy-done, bf16[1024,1024]{1,0:T(8,128)(2,1)} %param.28, bf16[512,1024]{1,0:T(8,128)(2,1)} %copy-done.3, f32[1024]{0:T(1024)S(1)} %convert_element_type.119, f32[512]{0:T(512)S(1)} %add_rsqrt_fusion, f32[512]{0:T(512)S(1)} %broadcast_multiply_fusion), kind=kOutput, calls=%fused_computation.57 | convolution fusion | flops 2155347968 | bytes 6299648 | tf_op jit(solution)/shard_map/dot_general | solution.py:179
  164.6 25.4 %reduce-scatter.2.cloned.1.call-done = bf16[512,256]{1,0:T(8,128)(2,1)} async-done(((bf16[512,1024]{1,0:T(8,128)(2,1)}), bf16[512,256]{1,0:T(8,128)(2,1)}) %reduce-scatter.2.cloned.1.call-update) | async-done | bytes 262160 | tf_op jit(solution)/shard_map/reduce_scatter | solution.py:180
  190.0 1.8 add_convert_fusion
  (66 shorter events, 16.5 us)
Async XLA Ops:
  6.5 152.7 %copy-start = (bf16[1024,1024]{1,0:T(8,128)(2,1)S(1)}, bf16[1024,1024]{1,0:T(8,128)(2,1)}, u32[]{:S(2)}) copy-start(bf16[1024,1024]{1,0:T(8,128)(2,1)} %param.29) | copy-start | bytes 6291460
  6.5 34.3 %all-gather.3.cloned.1.call-start = ((), (), s32[]{:S(2)}) async-start(), calls=%async_computation.1 | async-start | bytes 1310720 | tf_op jit(solution)/shard_map/all_gather | solution.py:100
  7.5 13.0 %collective-permute-start.1 = (bf16[64,256]{1,0:T(8,128)(2,1)S(1)}, bf16[64,256]{1,0:T(8,128)(2,1)S(1)}, u32[]{:S(2)}, u32[]{:S(2)}) collective-permute-start(bf16[64,256]{1,0:T(8,128)(2,1)S(1)} %get-tuple-element.344), channel_id=1, source_target_pairs={{4,0},{8,4},{12,8},{5,1},{9,5},{13,9},{6,2},{10,6},{14,10},{7,3},{... | collective-permute-start | bytes 98312 | tf_op jit(solution)/shard_map/ppermute | solution.py:24
  8.8 11.7 %collective-permute-start = (bf16[64,256]{1,0:T(8,128)(2,1)S(1)}, bf16[64,256]{1,0:T(8,128)(2,1)S(1)}, u32[]{:S(2)}, u32[]{:S(2)}) collective-permute-start(bf16[64,256]{1,0:T(8,128)(2,1)S(1)} %get-tuple-element.343), channel_id=1, source_target_pairs={{0,4},{4,8},{8,12},{1,5},{5,9},{9,13},{2,6},{6,10},{10,14},{3,7},{... | collective-permute-start | bytes 98312 | tf_op jit(solution)/shard_map/ppermute | solution.py:23
  20.8 1.6 copy-start.4
  20.8 2.5 %copy-start.5 = (bf16[1024]{0:T(1024)(128)(2,1)S(1)}, bf16[1024]{0:T(1024)(128)(2,1)}, u32[]{:S(2)}) copy-start(bf16[1024]{0:T(1024)(128)(2,1)} %param.22) | copy-start | bytes 6148
  23.2 70.4 %all-gather.5.cloned.1.call-start = ((), (), s32[]{:S(2)}) async-start(), calls=%async_computation.2 | async-start | bytes 2621440 | tf_op jit(solution)/shard_map/all_gather | solution.py:10
  40.9 3.2 %copy-start.1 = (bf16[512,1024]{1,0:T(8,128)(2,1)S(1)}, bf16[512,1024]{1,0:T(8,128)(2,1)}, u32[]{:S(2)}) copy-start(bf16[512,1024]{1,0:T(8,128)(2,1)} %all-gather.3.cloned.1.call-done) | copy-start | bytes 3145732
  42.4 3.5 %copy-start.7 = (bf16[1024,256]{1,0:T(8,128)(2,1)S(1)}, bf16[1024,256]{1,0:T(8,128)(2,1)}, u32[]{:S(2)}) copy-start(bf16[1024,256]{1,0:T(8,128)(2,1)} %param.24) | copy-start | bytes 1572868
  47.5 108.7 %all-reduce.3.cloned.1.call-start = ((), (), s32[]{:S(2)}) async-start(), calls=%async_computation.3 | async-start | bytes 2097152 | tf_op jit(solution)/shard_map/psum | solution.py:170
  118.5 2.8 %copy-start.6 = (bf16[1024]{0:T(1024)(128)(2,1)S(1)}, bf16[1024]{0:T(1024)(128)(2,1)}, u32[]{:S(2)}) copy-start(bf16[1024]{0:T(1024)(128)(2,1)} %param.27) | copy-start | bytes 6148
  118.6 37.6 %copy-start.2 = (bf16[512,1024]{1,0:T(8,128)(2,1)S(1)}, bf16[512,1024]{1,0:T(8,128)(2,1)}, u32[]{:S(2)}) copy-start(bf16[512,1024]{1,0:T(8,128)(2,1)} %all-gather.3.cloned.1.call-done) | copy-start | bytes 3145732
  121.2 68.8 %reduce-scatter.2.cloned.1.call-start = ((), (), s32[]{:S(2)}) async-start(), calls=%async_computation.4 | async-start | bytes 1310720 | tf_op jit(solution)/shard_map/reduce_scatter | solution.py:180
  157.8 1.0 copy-start.3
Sparse Core Ops, SparseCore 0:
  23.3 17.5 all-gather.2
  47.6 45.9 all-gather.4
  121.3 34.8 all-reduce.2
  164.7 25.2 reduce-scatter.1
